TPU v7x, 512 devices: a whole 4x4x16 slice. The times are simulated.
512 devices in a mesh: seq: 32 (over x, y, core), mp: 16 (over z).
Axes of the slice: x: 4, y: 4, z: 16, core: 2. Of those that a mesh axis runs over, the one named last changes fastest.
Arguments:
- token_ids: int32 [256, 4], replicated, may hold values from 0 to 151935
- embedding: bfloat16 [151936, 1536], P('seq', 'mp'), may hold values from -13 to 13
- attn_gain: float32 [1536], P('mp'), may hold values from 0.25 to 1.75
- w_qkv: bfloat16 [1536, 2048], P('mp', 'seq'), may hold values from -0.15625 to 0.15625
- w_out: bfloat16 [1536, 1536], P('seq', 'mp'), may hold values from -0.15625 to 0.15625
- prompt_cache: bfloat16 [2, 32, 2048, 256], P(None, 'mp', 'seq'), may hold values from -170 to 170
- request_cache: bfloat16 [2, 256, 2048, 256], P(None, 'mp', 'seq'), may hold values from -170 to 170
- group_ids: int32 [256], P('mp'), may hold values from 0 to 1
- prefix_len: int32 [32], P('mp'), may hold values from 1 to 2048
- suffix_len: int32 [256], P('mp'), may hold values from 0 to 2048
- moe_gain: float32 [1536], replicated, may hold values from 0.25 to 1.75
- w_router: bfloat16 [1536, 32], replicated, may hold values from -0.15625 to 0.15625
- w_gate_up: bfloat16 [32, 2, 768, 1536], P('seq', None, 'mp'), may hold values from -0.15625 to 0.15625
- w_down: bfloat16 [32, 768, 1536], P('seq', 'mp'), may hold values from -0.21875 to 0.21875
- routes: int32 [256, 4, 4], replicated, may hold values from 0 to 31, all different within a row; in each aligned block of 32 rows (0 to 31, 32 to 63, ..., all dimensions but the last counted through in order) at most 8 rows name the same one
Outputs:
- hidden_out: bfloat16 [256, 4, 1536], P('seq', None, 'mp')
Inputs may be any that keep to these rules, and one draw needn't show every extreme that they name: `routes`: in each aligned block of 32 rows (request, step) taken in order, the requests of one index of seq, no expert is named more than 8 times.
All inputs are finite; a program needn't handle non-finite values.
Results may differ from a plain program's by a relative error of at most 0.015.
The roundings to bfloat16 on the way count: a program that leaves them out, or rounds other values in their place, can miss the bound.
Values may be sent and summed in bfloat16 or wider, within the bound.
No kernel may reach another device: no remote copies, remote signals or barrier semaphores. Data moves between devices by JAX's collectives and lax.ppermute only.
A program may use at most 128 MiB of HBM per device.

v0:
```python
import math
import numpy as np
import jax
import jax.numpy as jnp
from jax import lax
from jax.sharding import PartitionSpec as P

D = 1536
QUERY_HEADS = 12
KEY_VALUE_HEADS = 2
HEAD_SIZE = 128
E = 32
TOPK = 4
NEW_TOKENS = 4
MOST = 8
EPS = 1e-06
NEG = -1e30


def exchange(values, axis):
    return lax.all_to_all(values, axis, 0, 0, tiled=True)


def on_device(
    token_ids,
    embedding,
    attn_gain,
    w_qkv,
    w_out,
    prompt_cache,
    request_cache,
    group_ids,
    prefix_len,
    suffix_len,
    moe_gain,
    w_router,
    w_gate_up,
    w_down,
    routes,
):
    n_seq = lax.axis_size("seq")
    n_mp = lax.axis_size("mp")
    s = lax.axis_index("seq")
    total_rows = token_ids.shape[0] * NEW_TOKENS
    home_rows = total_rows // n_seq
    feat_mp = embedding.shape[1]
    vocab_rows = embedding.shape[0]
    local_ids = token_ids.reshape(total_rows) - s * vocab_rows
    inside = (local_ids >= 0) & (local_ids < vocab_rows)
    looked = jnp.take(embedding, jnp.clip(local_ids, 0, vocab_rows - 1), axis=0)
    looked = jnp.where(inside[:, None], looked, jnp.zeros_like(looked))
    got = exchange(looked.reshape(n_seq, home_rows, feat_mp), "seq")
    x_home = jnp.sum(got.astype(jnp.float32), axis=0)
    square_sum = lax.psum(jnp.sum(x_home * x_home, axis=-1), "mp")
    normed = (x_home * lax.rsqrt(square_sum[:, None] / D + EPS) * attn_gain).astype(jnp.bfloat16)
    normed_all = lax.all_gather(normed, "seq", axis=0, tiled=True)
    qkv_part = jnp.dot(normed_all, w_qkv, preferred_element_type=jnp.float32)
    attn_rows = total_rows // n_mp
    qkv_got = exchange(qkv_part.reshape(n_mp, attn_rows, qkv_part.shape[-1]), "mp")
    qkv_cols = jnp.sum(qkv_got, axis=0).astype(jnp.bfloat16)
    qkv_rows = lax.all_gather(qkv_cols, "seq", axis=1, tiled=True)
    request_count = group_ids.shape[0]
    groups_per = QUERY_HEADS // KEY_VALUE_HEADS
    qf = QUERY_HEADS * HEAD_SIZE
    kf = KEY_VALUE_HEADS * HEAD_SIZE
    q = qkv_rows[:, :qf].reshape(request_count, NEW_TOKENS, KEY_VALUE_HEADS, groups_per, HEAD_SIZE)
    k_new = qkv_rows[:, qf : qf + kf].reshape(request_count, NEW_TOKENS, KEY_VALUE_HEADS, HEAD_SIZE)
    v_new = qkv_rows[:, qf + kf :].reshape(request_count, NEW_TOKENS, KEY_VALUE_HEADS, HEAD_SIZE)
    pre_rows = prompt_cache.shape[2]
    suf_rows = request_cache.shape[2]
    first_group = (group_ids == 0)[:, None, None]
    pre_k = jnp.where(first_group, prompt_cache[0, 0][None], prompt_cache[0, 1][None])
    pre_v = jnp.where(first_group, prompt_cache[1, 0][None], prompt_cache[1, 1][None])
    keys = jnp.concatenate([pre_k, request_cache[0]], axis=1).reshape(
        request_count, pre_rows + suf_rows, KEY_VALUE_HEADS, HEAD_SIZE
    )
    values = jnp.concatenate([pre_v, request_cache[1]], axis=1).reshape(
        request_count, pre_rows + suf_rows, KEY_VALUE_HEADS, HEAD_SIZE
    )
    own_prefix = jnp.where(group_ids == 0, prefix_len[0], prefix_len[1])
    pre_pos = s * pre_rows + jnp.arange(pre_rows, dtype=jnp.int32)
    suf_pos = s * suf_rows + jnp.arange(suf_rows, dtype=jnp.int32)
    valid = jnp.concatenate(
        [pre_pos[None, :] < own_prefix[:, None], suf_pos[None, :] < suffix_len[:, None]], axis=1
    )[:, None, None, None, :]
    score_scale = 1.0 / math.sqrt(HEAD_SIZE)
    scores = (
        jnp.einsum("jtkgd,jpkd->jtkgp", q, keys, preferred_element_type=jnp.float32) * score_scale
    )
    scores = jnp.where(valid, scores, NEG)
    block_max = jnp.max(scores, axis=-1)
    probs = jnp.where(valid, jnp.exp(scores - block_max[..., None]), 0.0)
    block_sum = jnp.sum(probs, axis=-1)
    block_acc = jnp.einsum(
        "jtkgp,jpkd->jtkgd", probs.astype(jnp.bfloat16), values, preferred_element_type=jnp.float32
    )
    new_scores = (
        jnp.einsum("jtkgd,jukd->jtkgu", q, k_new, preferred_element_type=jnp.float32) * score_scale
    )
    causal = (jnp.arange(NEW_TOKENS)[:, None] >= jnp.arange(NEW_TOKENS)[None, :])[
        None, :, None, None, :
    ]
    new_scores = jnp.where(causal, new_scores, NEG)
    new_max = jnp.max(new_scores, axis=-1)
    new_probs = jnp.where(causal, jnp.exp(new_scores - new_max[..., None]), 0.0)
    new_sum = jnp.sum(new_probs, axis=-1)
    new_acc = jnp.einsum(
        "jtkgu,jukd->jtkgd",
        new_probs.astype(jnp.bfloat16),
        v_new,
        preferred_element_type=jnp.float32,
    )
    fs = qf // n_seq
    acc_flat = block_acc.reshape(attn_rows, qf)
    acc_parts = acc_flat.reshape(attn_rows, n_seq, fs).transpose(1, 0, 2)
    head_pick = np.array(
        [[i * fs // HEAD_SIZE, (i * fs + fs - 1) // HEAD_SIZE] for i in range(n_seq)]
    )
    max_flat = block_max.reshape(attn_rows, QUERY_HEADS)
    sum_flat = block_sum.reshape(attn_rows, QUERY_HEADS)
    max_parts = max_flat[:, head_pick].transpose(1, 0, 2)
    sum_parts = sum_flat[:, head_pick].transpose(1, 0, 2)
    merged = exchange(jnp.concatenate([acc_parts, max_parts, sum_parts], axis=-1), "seq")
    got_acc = merged[..., :fs]
    feat_ids = s * fs + jnp.arange(fs, dtype=jnp.int32)
    second = feat_ids // HEAD_SIZE - s * fs // HEAD_SIZE == 1
    got_max = jnp.where(second, merged[..., fs + 1 : fs + 2], merged[..., fs : fs + 1])
    got_sum = jnp.where(second, merged[..., fs + 3 : fs + 4], merged[..., fs + 2 : fs + 3])
    own_heads = feat_ids // HEAD_SIZE
    n_max = jnp.take(new_max.reshape(attn_rows, QUERY_HEADS), own_heads, axis=1)
    n_sum = jnp.take(new_sum.reshape(attn_rows, QUERY_HEADS), own_heads, axis=1)
    n_acc = lax.dynamic_slice_in_dim(new_acc.reshape(attn_rows, qf), s * fs, fs, 1)
    overall = jnp.maximum(jnp.max(got_max, axis=0), n_max)
    cache_weight = jnp.exp(got_max - overall)
    own_weight = jnp.exp(n_max - overall)
    denominator = jnp.sum(cache_weight * got_sum, axis=0) + own_weight * n_sum
    numerator = jnp.sum(cache_weight * got_acc, axis=0) + own_weight * n_acc
    attended = (numerator / denominator).astype(jnp.bfloat16)
    att_all = lax.all_gather(attended, "mp", axis=0, tiled=True)
    out_part = jnp.dot(att_all, w_out, preferred_element_type=jnp.float32)
    out_got = exchange(out_part.reshape(n_seq, home_rows, out_part.shape[-1]), "seq")
    x2 = (x_home + jnp.sum(out_got, axis=0)).astype(jnp.bfloat16)
    route_blocks = routes.reshape(n_seq, home_rows, TOPK)
    experts_all = jnp.arange(E, dtype=jnp.int32)
    hit = jnp.any(route_blocks[:, :, :, None] == experts_all, axis=2)
    hit_count = hit.astype(jnp.int32)
    ahead = jnp.cumsum(hit_count, axis=1) - hit_count
    chosen = hit[..., None] & (ahead[..., None] == jnp.arange(MOST, dtype=jnp.int32))
    chosen = jnp.transpose(chosen, (0, 2, 3, 1)).astype(jnp.bfloat16)
    member = hit.astype(jnp.bfloat16)
    home_table = chosen[s]
    dispatch = jnp.einsum("esr,rf->esf", home_table, x2, preferred_element_type=jnp.float32).astype(
        jnp.bfloat16
    )
    slot_rows = exchange(dispatch, "seq")
    slot_full = lax.all_gather(slot_rows, "mp", axis=2, tiled=True).reshape(n_seq * MOST, D)
    expert = s
    expert_table = chosen[:, expert]
    slot_member = jnp.einsum(
        "bsr,bre->bse", expert_table, member, preferred_element_type=jnp.float32
    ).reshape(n_seq * MOST, E)
    floats2 = slot_full.astype(jnp.float32)
    mean_sq = jnp.mean(floats2 * floats2, axis=-1, keepdims=True)
    normed2 = (floats2 * lax.rsqrt(mean_sq + EPS) * moe_gain).astype(jnp.bfloat16)
    logits = jnp.dot(normed2, w_router, preferred_element_type=jnp.float32)
    which = (experts_all == expert).astype(jnp.float32)
    own_flag = jnp.sum(slot_member * which, axis=1)
    own_logit = jnp.sum(logits * which, axis=1)
    denom = jnp.sum(jnp.where(slot_member > 0, jnp.exp(logits), 0.0), axis=1)
    share = own_flag * jnp.exp(own_logit) / (denom + 1.0 - own_flag)
    gate_up = w_gate_up[0]
    half = gate_up.shape[1]
    both = lax.dot_general(
        normed2,
        gate_up.reshape(2 * half, D),
        (((1,), (1,)), ((), ())),
        preferred_element_type=jnp.float32,
    )
    hidden = (jnp.maximum(both[:, :half], 0.0) * both[:, half:]).astype(jnp.bfloat16)
    down_part = jnp.dot(hidden, w_down[0], preferred_element_type=jnp.float32).astype(jnp.bfloat16)
    down_got = exchange(down_part.reshape(n_seq * MOST, n_mp, feat_mp).transpose(1, 0, 2), "mp")
    expert_out = jnp.sum(down_got.astype(jnp.float32), axis=0).astype(jnp.bfloat16)
    weighted = (share[:, None] * expert_out.astype(jnp.float32)).astype(jnp.bfloat16)
    back = exchange(weighted.reshape(n_seq, MOST, feat_mp), "seq")
    terms = jnp.einsum("esr,esf->rf", home_table, back, preferred_element_type=jnp.float32)
    final = (x2.astype(jnp.float32) + terms).astype(jnp.bfloat16)
    return final.reshape(home_rows // NEW_TOKENS, NEW_TOKENS, feat_mp)


def solution(mesh):
    in_specs = (
        P(),
        P("seq", "mp"),
        P("mp"),
        P("mp", "seq"),
        P("seq", "mp"),
        P(None, "mp", "seq", None),
        P(None, "mp", "seq", None),
        P("mp"),
        P("mp"),
        P("mp"),
        P(),
        P(),
        P("seq", None, "mp", None),
        P("seq", "mp", None),
        P(),
    )
    out_specs = P("seq", None, "mp")
    return jax.shard_map(
        on_device, mesh=mesh, in_specs=in_specs, out_specs=out_specs, check_vma=False
    )
```

profile of v0, /device:TPU:1, one launch (start us, length us, event | category | flops | bytes accessed | tf_op | source)
XLA Modules:
  0.0 341.7 jit_solution(17688282065486856965)
XLA Ops:
  0.0 0.7 compare_and_fusion.1
  0.7 0.7 subtract_clamp_fusion
  2.2 2.2 copy.150
  4.4 3.2 gather_fusion
  7.6 1.0 select_select_fusion
  8.6 10.5 %all-to-all-start = ((bf16[32,32,96]{2,1,0:T(8,128)(2,1)}), bf16[32,32,96]{2,1,0:T(8,128)(2,1)S(1)}, u32[]{:S(2)}, u32[]{:S(2)}) async-start(bf16[32,32,96]{2,1,0:T(8,128)(2,1)} %select_select_fusion), calls=%async_computation | async-start | bytes 524288 | tf_op jit(solution)/shard_map/all_to_all | solution.py:21
  19.1 0.6 iota_compare_fusion.2
  19.7 0.6 compare_and_fusion.2
  20.8 0.8 fusion.1
  21.6 1.1 copy.194
  22.8 0.6 subtract_compare_fusion
  23.4 0.5 fusion.75
  24.2 1.3 copy.196
  26.4 1.2 broadcast_select_fusion.2
  27.6 0.6 all-to-all-done
  28.4 27.4 %psum.7 = f32[32]{0:T(128)S(1)} all-reduce(f32[32]{0:T(128)S(1)} %multiply_reduce_fusion.2), channel_id=1, replica_groups=mesh['seq'=32,'mp'=16] {'mp'}, use_global_device_ids=true, to_apply=%region_2.3 | all-reduce | flops 32 | bytes 256 | tf_op jit(solution)/shard_map/psum | solution.py:54
  55.8 32.0 %all_gather.12 = bf16[1024,96]{1,0:T(8,128)(2,1)S(1)} all-gather(bf16[32,96]{1,0:T(8,128)(2,1)S(1)} %multiply_convert_fusion), channel_id=1, replica_groups=mesh['seq'=32,'mp'=16] {'seq'}, dimensions={0}, use_global_device_ids=true | all-gather | bytes 202752 | tf_op jit(solution)/shard_map/all_gather | solution.py:56
  88.4 1.0 reshape.313
  89.5 6.4 %all-to-all-start.1 = ((f32[16,1,4096]{2,1,0:T(1,128)}), f32[16,1,4096]{2,1,0:T(1,128)S(1)}, u32[]{:S(2)}, u32[]{:S(2)}) async-start(f32[16,1,4096]{2,1,0:T(1,128)} %reshape.313), calls=%async_computation.1 | async-start | bytes 524288 | tf_op jit(solution)/shard_map/all_to_all | solution.py:21
  96.0 0.6 pad_clamp_fusion
  96.8 13.2 %all-to-all-done.1 = f32[16,1,4096]{2,1,0:T(1,128)S(1)} async-done(((f32[16,1,4096]{2,1,0:T(1,128)}), f32[16,1,4096]{2,1,0:T(1,128)S(1)}, u32[]{:S(2)}, u32[]{:S(2)}) %all-to-all-start.1) | async-done | bytes 262176 | tf_op jit(solution)/shard_map/all_to_all | solution.py:21
  110.0 0.5 broadcast.250
  110.5 1.2 reduce.3
  111.9 29.1 %all_gather.13 = bf16[64,2048]{0,1:T(8,128)(2,1)S(1)} all-gather(bf16[64,64]{0,1:T(8,128)(2,1)S(1)} %bitcast_reduce_fusion), channel_id=1, replica_groups=mesh['seq'=32,'mp'=16] {'seq'}, dimensions={1}, use_global_device_ids=true | all-gather | bytes 270336 | tf_op jit(solution)/shard_map/all_gather | solution.py:61
  141.4 0.6 reshape.243
  142.3 0.8 fusion.76
  143.3 0.5 fusion.34
  143.8 0.4 convolution_bitcast_fusion.1
  144.8 0.6 gather_fusion.1
  145.4 0.6 gather_fusion.2
  146.0 0.4 reshape_reshape.3
  146.5 1.0 copy.167
  147.4 1.0 copy.164
  148.4 1.6 pad_maximum_fusion
  150.0 1.8 copy.168
  151.9 1.3 reshape.315
  153.2 4.4 %all-to-all-start.2 = ((f32[32,1,3328]{2,1,0:T(1,128)}), f32[32,1,3328]{2,1,0:T(1,128)S(1)}, u32[]{:S(2)}, u32[]{:S(2)}) async-start(f32[32,1,3328]{2,1,0:T(1,128)} %reshape.315), calls=%async_computation.2 | async-start | bytes 851968 | tf_op jit(solution)/shard_map/all_to_all | solution.py:21
  157.6 1.3 fusion.77
  160.2 0.7 gather_fusion.4
  160.9 0.7 gather_fusion.3
  161.6 0.3 convolution_bitcast_fusion
  162.2 5.9 %all-to-all-done.2 = f32[32,1,3328]{2,1,0:T(1,128)S(1)} async-done(((f32[32,1,3328]{2,1,0:T(1,128)}), f32[32,1,3328]{2,1,0:T(1,128)S(1)}, u32[]{:S(2)}, u32[]{:S(2)}) %all-to-all-start.2) | async-done | bytes 426016 | tf_op jit(solution)/shard_map/all_to_all | solution.py:21
  168.2 1.5 reduce.4
  170.3 0.4 fusion.21
  170.8 24.4 %all-gather = bf16[16,64,48]{1,2,0:T(8,128)(2,1)S(1)} all-gather(bf16[1,64,48]{1,2,0:T(8,128)(2,1)S(1)} %fusion.63), channel_id=1, replica_groups=mesh['seq'=32,'mp'=16] {'mp'}, dimensions={0}, use_global_device_ids=true | all-gather | bytes 104448 | tf_op jit(solution)/shard_map/all_gather | solution.py:139
  195.5 1.1 fusion.79
  196.6 10.6 %all-to-all-start.3 = ((f32[32,32,96]{2,1,0:T(8,128)}), f32[32,32,96]{2,1,0:T(8,128)S(1)}, u32[]{:S(2)}, u32[]{:S(2)}) async-start(f32[32,32,96]{2,1,0:T(8,128)} %bitcast.26), calls=%async_computation.3 | async-start | bytes 1048576 | tf_op jit(solution)/shard_map/all_to_all | solution.py:21
  207.3 0.9 fusion
  208.2 0.9 copy-done.5
  209.3 9.6 %all-to-all-done.3 = f32[32,32,96]{2,1,0:T(8,128)S(1)} async-done(((f32[32,32,96]{2,1,0:T(8,128)}), f32[32,32,96]{2,1,0:T(8,128)S(1)}, u32[]{:S(2)}, u32[]{:S(2)}) %all-to-all-start.3) | async-done | bytes 393248 | tf_op jit(solution)/shard_map/all_to_all | solution.py:21
  219.2 10.8 %all_to_all.35 = bf16[32,8,96]{2,1,0:T(8,128)(2,1)S(1)} all-to-all(bf16[32,8,96]{2,1,0:T(8,128)(2,1)S(1)} %copy.198), channel_id=1, replica_groups=mesh['seq'=32,'mp'=16] {'seq'}, dimensions={0} | all-to-all | bytes 98304 | tf_op jit(solution)/shard_map/all_to_all | solution.py:21
  229.9 0.8 copy.199
  230.8 45.7 %all_gather.15 = bf16[32,8,1536]{0,1,2:T(8,128)(2,1)S(1)} all-gather(bf16[32,8,96]{0,1,2:T(8,128)(2,1)} %copy.199), channel_id=1, replica_groups=mesh['seq'=32,'mp'=16] {'mp'}, dimensions={2}, use_global_device_ids=true | all-gather | bytes 835584 | tf_op jit(solution)/shard_map/all_gather | solution.py:156
  276.5 3.6 %copy.200 = bf16[32,8,1536]{2,1,0:T(8,128)(2,1)} copy(bf16[32,8,1536]{0,1,2:T(8,128)(2,1)S(1)} %all_gather.15) | data formatting | bytes 1572864 | tf_op jit(solution)/shard_map/all_gather | solution.py:156
  280.1 1.4 fusion.5
  281.7 1.6 fusion.24
  283.3 0.4 convolution_convert_fusion
  283.7 1.2 copy.205
  284.9 5.1 %all-to-all-start.5 = ((bf16[16,256,96]{1,2,0:T(8,128)(2,1)}), bf16[16,256,96]{1,2,0:T(8,128)(2,1)S(1)}, u32[]{:S(2)}, u32[]{:S(2)}) async-start(bf16[16,256,96]{1,2,0:T(8,128)(2,1)} %bitcast.39), calls=%async_computation.5 | async-start | bytes 1572864 | tf_op jit(solution)/shard_map/all_to_all | solution.py:21
  290.0 1.0 multiply_reduce_fusion
  291.3 0.4 multiply_reduce_fusion.1
  292.0 29.6 %all-to-all-done.5 = bf16[16,256,96]{1,2,0:T(8,128)(2,1)S(1)} async-done(((bf16[16,256,96]{1,2,0:T(8,128)(2,1)}), bf16[16,256,96]{1,2,0:T(8,128)(2,1)S(1)}, u32[]{:S(2)}, u32[]{:S(2)}) %all-to-all-start.5) | async-done | bytes 786464 | tf_op jit(solution)/shard_map/all_to_all | solution.py:21
  321.8 19.1 %all_to_all.36 = bf16[32,8,96]{2,1,0:T(8,128)(2,1)S(1)} all-to-all(bf16[32,8,96]{2,1,0:T(8,128)(2,1)S(1)} %fusion.46), channel_id=1, replica_groups=mesh['seq'=32,'mp'=16] {'seq'}, dimensions={0} | all-to-all | bytes 98304 | tf_op jit(solution)/shard_map/all_to_all | solution.py:21
  340.9 0.8 fusion.13
  (142 shorter events, 8.8 us)
Async XLA Ops:
  0.0 281.7 %copy-start = (bf16[1,2,48,1536]{3,2,1,0:T(8,128)(2,1)S(1)}, bf16[1,2,48,1536]{3,2,1,0:T(8,128)(2,1)}, u32[]{:S(2)}) copy-start(bf16[1,2,48,1536]{3,2,1,0:T(8,128)(2,1)} %param.32) | copy-start | bytes 884740
  4.4 16.0 %copy-start.13 = (s32[256,4,4]{0,2,1:T(4,128)S(1)}, s32[256,4,4]{0,2,1:T(4,128)}, u32[]{:S(2)}) copy-start(s32[256,4,4]{0,2,1:T(4,128)} %param.34) | copy-start | bytes 49156
  8.6 14.8 %copy-start.19 = (s32[2]{0:T(128)S(1)}, s32[2]{0:T(128)}, u32[]{:S(2)}) copy-start(s32[2]{0:T(128)} %param.28) | copy-start | bytes 28
  8.6 15.4 %copy-start.11 = (bf16[2,2,64,256]{3,2,1,0:T(8,128)(2,1)S(1)}, bf16[2,2,64,256]{3,2,1,0:T(8,128)(2,1)}, u32[]{:S(2)}) copy-start(bf16[2,2,64,256]{3,2,1,0:T(8,128)(2,1)} %param.25) | copy-start | bytes 393220
  8.6 19.6 %all-to-all-start = ((bf16[32,32,96]{2,1,0:T(8,128)(2,1)}), bf16[32,32,96]{2,1,0:T(8,128)(2,1)S(1)}, u32[]{:S(2)}, u32[]{:S(2)}) async-start(bf16[32,32,96]{2,1,0:T(8,128)(2,1)} %select_select_fusion), calls=%async_computation | async-start | bytes 524288 | tf_op jit(solution)/shard_map/all_to_all | solution.py:21
  20.7 4.7 %copy-start.6 = (bf16[2,16,64,256]{3,2,1,0:T(8,128)(2,1)S(1)}, bf16[2,16,64,256]{3,2,1,0:T(8,128)(2,1)}, u32[]{:S(2)}) copy-start(bf16[2,16,64,256]{3,2,1,0:T(8,128)(2,1)} %param.26) | copy-start | bytes 3145732
  21.6 2.6 copy-start.3
  25.7 0.7 copy-start.22
  25.8 30.0 %copy-start.20 = (f32[96]{0:T(128)S(1)}, f32[96]{0:T(128)}, u32[]{:S(2)}) copy-start(f32[96]{0:T(128)} %param.22) | copy-start | bytes 1156
  25.9 62.0 %copy-start.14 = (bf16[96,64]{0,1:T(8,128)(2,1)S(1)}, bf16[96,64]{0,1:T(8,128)(2,1)}, u32[]{:S(2)}) copy-start(bf16[96,64]{0,1:T(8,128)(2,1)} %param.23) | copy-start | bytes 36868
  88.1 7.8 %copy-start.23 = (s32[16]{0:T(128)S(1)}, s32[16]{0:T(128)}, u32[]{:S(2)}) copy-start(s32[16]{0:T(128)} %param.29) | copy-start | bytes 196
  88.1 8.5 %copy-start.21 = (s32[64]{0:T(128)S(1)}, s32[64]{0:T(128)}, u32[]{:S(2)}) copy-start(s32[64]{0:T(128)} %constant.117) | copy-start | bytes 772
  89.5 20.6 %all-to-all-start.1 = ((f32[16,1,4096]{2,1,0:T(1,128)}), f32[16,1,4096]{2,1,0:T(1,128)S(1)}, u32[]{:S(2)}, u32[]{:S(2)}) async-start(f32[16,1,4096]{2,1,0:T(1,128)} %reshape.313), calls=%async_computation.1 | async-start | bytes 524288 | tf_op jit(solution)/shard_map/all_to_all | solution.py:21
  142.2 1.6 copy-start.8
  151.9 5.7 %copy-start.9 = (bf16[16,4,2,6,128]{4,3,2,1,0:T(8,128)(2,1)S(1)}, bf16[16,4,2,6,128]{4,3,2,1,0:T(8,128)(2,1)}, u32[]{:S(2)}) copy-start(bf16[16,4,2,6,128]{4,3,2,1,0:T(8,128)(2,1)} %copy-done.8) | copy-start | bytes 589828
  151.9 5.7 %copy-start.12 = (bf16[16,4,2,128]{3,2,1,0:T(2,128)(2,1)S(1)}, bf16[16,4,2,128]{3,2,1,0:T(2,128)(2,1)}, u32[]{:S(2)}) copy-start(bf16[16,4,2,128]{3,2,1,0:T(2,128)(2,1)} %reshape.243) | copy-start | bytes 98308
  151.9 5.7 %copy-start.17 = (pred[4,4]{1,0:T(4,128)(4,1)S(1)}, pred[4,4]{1,0:T(4,128)(4,1)}, u32[]{:S(2)}) copy-start(pred[4,4]{1,0:T(4,128)(4,1)} %iota_compare_fusion.2) | copy-start | bytes 52
  153.2 15.0 %all-to-all-start.2 = ((f32[32,1,3328]{2,1,0:T(1,128)}), f32[32,1,3328]{2,1,0:T(1,128)S(1)}, u32[]{:S(2)}, u32[]{:S(2)}) async-start(f32[32,1,3328]{2,1,0:T(1,128)} %reshape.315), calls=%async_computation.2 | async-start | bytes 851968 | tf_op jit(solution)/shard_map/all_to_all | solution.py:21
  162.0 8.1 %copy-start.18 = (pred[48]{0:T(512)(128)(4,1)S(1)}, pred[48]{0:T(512)(128)(4,1)}, u32[]{:S(2)}) copy-start(pred[48]{0:T(512)(128)(4,1)} %subtract_compare_fusion) | copy-start | bytes 148
  162.0 8.3 %copy-start.16 = (pred[48]{0:T(512)(128)(4,1)S(1)}, pred[48]{0:T(512)(128)(4,1)}, u32[]{:S(2)}) copy-start(pred[48]{0:T(512)(128)(4,1)} %compare_and_fusion.2) | copy-start | bytes 148
  169.7 25.8 %copy-start.15 = (bf16[48,96]{1,0:T(8,128)(2,1)S(1)}, bf16[48,96]{1,0:T(8,128)(2,1)}, u32[]{:S(2)}) copy-start(bf16[48,96]{1,0:T(8,128)(2,1)} %param.24) | copy-start | bytes 27652
  170.7 36.5 %copy-start.2 = (s32[32,32,32]{1,0,2:T(8,128)S(1)}, s32[32,32,32]{1,0,2:T(8,128)}, u32[]{:S(2)}) copy-start(s32[32,32,32]{1,0,2:T(8,128)} %copy.196) | copy-start | bytes 393220
  170.7 36.5 %copy-start.7 = (pred[32,32,32]{1,0,2:T(8,128)(4,1)S(1)}, pred[32,32,32]{1,0,2:T(8,128)(4,1)}, u32[]{:S(2)}) copy-start(pred[32,32,32]{1,0,2:T(8,128)(4,1)} %copy.194) | copy-start | bytes 98308
  196.6 22.2 %all-to-all-start.3 = ((f32[32,32,96]{2,1,0:T(8,128)}), f32[32,32,96]{2,1,0:T(8,128)S(1)}, u32[]{:S(2)}, u32[]{:S(2)}) async-start(f32[32,32,96]{2,1,0:T(8,128)} %bitcast.26), calls=%async_computation.3 | async-start | bytes 1048576 | tf_op jit(solution)/shard_map/all_to_all | solution.py:21
  208.2 1.0 copy-start.5
  276.5 5.2 %copy-start.25 = (f32[1536]{0:T(1024)S(1)}, f32[1536]{0:T(1024)}, u32[]{:S(2)}) copy-start(f32[1536]{0:T(1024)} %param.30) | copy-start | bytes 18436
  280.1 3.2 copy-start.10
  283.7 6.3 %copy-start.4 = (pred[32,32,32]{2,1,0:T(8,128)(4,1)S(1)}, pred[32,32,32]{2,1,0:T(8,128)(4,1)}, u32[]{:S(2)}) copy-start(pred[32,32,32]{2,1,0:T(8,128)(4,1)} %copy-done.3) | copy-start | bytes 98308
  283.7 7.6 %copy-start.1 = (bf16[32,8,1536]{2,1,0:T(8,128)(2,1)S(1)}, bf16[32,8,1536]{2,1,0:T(8,128)(2,1)}, u32[]{:S(2)}) copy-start(bf16[32,8,1536]{2,1,0:T(8,128)(2,1)} %copy.200) | copy-start | bytes 2359300
  283.7 7.6 %copy-start.24 = (bf16[1536,32]{0,1:T(8,128)(2,1)S(1)}, bf16[1536,32]{0,1:T(8,128)(2,1)}, u32[]{:S(2)}) copy-start(bf16[1536,32]{0,1:T(8,128)(2,1)} %param.31) | copy-start | bytes 294916
  284.9 36.6 %all-to-all-start.5 = ((bf16[16,256,96]{1,2,0:T(8,128)(2,1)}), bf16[16,256,96]{1,2,0:T(8,128)(2,1)S(1)}, u32[]{:S(2)}, u32[]{:S(2)}) async-start(bf16[16,256,96]{1,2,0:T(8,128)(2,1)} %bitcast.39), calls=%async_computation.5 | async-start | bytes 1572864 | tf_op jit(solution)/shard_map/all_to_all | solution.py:21
where the time goes:
time: 343 us; the launch traced here: 342 us
  blocking collectives  189 us (55%)
  waiting for transfers between devices  58.9 us (17%)
  starting transfers between devices  37.1 us (11%)
  local copies, waits for them, and re-layouts  31.9 us (9%)
  other arithmetic  15.9 us (5%)
  matrix products  8.57 us (2%)
    all_to_all x5, waiting for transfers between devices, exchange(): return lax.all_to_all(values, axis, 0, 0, tiled=True)  58.9 us
    all_gather x1, blocking collectives, on_device(): lax.all_gather(slot_rows, 'mp', axis=2, tiled=True).reshape(n_seq * MOST, D)  45.7 us
    all_to_all x5, starting transfers between devices, exchange(): return lax.all_to_all(values, axis, 0, 0, tiled=True)  37.1 us
    all_gather x1, blocking collectives, on_device(): normed_all = lax.all_gather(normed, 'seq', axis=0, tiled=True)  32 us
    all_to_all x2, blocking collectives, exchange(): return lax.all_to_all(values, axis, 0, 0, tiled=True)  29.8 us
    all_gather x1, blocking collectives, on_device(): qkv_rows = lax.all_gather(qkv_cols, 'seq', axis=1, tiled=True)  29.1 us
    psum x1, blocking collectives, on_device(): square_sum = lax.psum(jnp.sum(x_home * x_home, axis=-1), 'mp')  27.4 us
    all_gather x1, blocking collectives, on_device(): att_all = lax.all_gather(attended, 'mp', axis=0, tiled=True)  24.4 us
  transfers between devices with their start and end apart: 5, of which 5 were waited for; matrix products, arithmetic and copies ran while one was open for 5% of the time, Pallas kernels for 0%

commit v1 on v0

--- a/solution.py
+++ b/solution.py
@@ -136,7 +136,16 @@
     denominator = jnp.sum(cache_weight * got_sum, axis=0) + own_weight * n_sum
     numerator = jnp.sum(cache_weight * got_acc, axis=0) + own_weight * n_acc
     attended = (numerator / denominator).astype(jnp.bfloat16)
-    att_all = lax.all_gather(attended, "mp", axis=0, tiled=True)
+    pair_strings_over_axis = lambda d_out, mine_x: jnp.concatenate(
+        lax.all_to_all(
+            jnp.stack([mine_x for _ in range(lax.axis_size("mp"))], 0),
+            concat_axis=0,
+            axis_name="mp",
+            split_axis=0,
+        ),
+        axis=d_out,
+    )
+    att_all = pair_strings_over_axis(0, attended)
     out_part = jnp.dot(att_all, w_out, preferred_element_type=jnp.float32)
     out_got = exchange(out_part.reshape(n_seq, home_rows, out_part.shape[-1]), "seq")
     x2 = (x_home + jnp.sum(out_got, axis=0)).astype(jnp.bfloat16)

time: 343 us -> 331 us (0.965)
  blocking collectives: 189 us -> 163 us
  waiting for transfers between devices: 58.9 us -> 72.6 us
    all_gather x1 -> x0, blocking collectives: 24.4 us -> none  [on_device(): att_all = lax.all_gather(attended, 'mp', axis=0, tiled=True)]
    all_to_all x0 -> x1, waiting for transfers between devices: none -> 10.2 us  [on_device(): lax.all_to_all(jnp.stack([mine_x for _ in range(lax.axis_size('mp'))], 0)...]
    all_to_all x5, starting transfers between devices: 37.1 us -> 30.5 us  [exchange(): return lax.all_to_all(values, axis, 0, 0, tiled=True)]
    all_to_all x0 -> x1, starting transfers between devices: none -> 5.83 us  [on_device(): lax.all_to_all(jnp.stack([mine_x for _ in range(lax.axis_size('mp'))], 0)...]
    all_to_all x5, waiting for transfers between devices: 58.9 us -> 62.3 us  [exchange(): return lax.all_to_all(values, axis, 0, 0, tiled=True)]
  transfers between devices with their start and end apart: 5 -> 6, of which waited for: 5 -> 6; matrix products, arithmetic and copies ran while one was open for 5% -> 5% of each run, Pallas kernels for 0% -> 0%
where the time goes in v1:
time: 331 us; the launch traced here: 329 us
  blocking collectives  163 us (49%)
  waiting for transfers between devices  72.6 us (22%)
  starting transfers between devices  36.3 us (11%)
  local copies, waits for them, and re-layouts  32.3 us (10%)
  other arithmetic  16 us (5%)
  matrix products  8.53 us (3%)
    all_to_all x5, waiting for transfers between devices, exchange(): return lax.all_to_all(values, axis, 0, 0, tiled=True)  62.3 us
    all_gather x1, blocking collectives, on_device(): lax.all_gather(slot_rows, 'mp', axis=2, tiled=True).reshape(n_seq * MOST, D)  46.6 us
    all_to_all x5, starting transfers between devices, exchange(): return lax.all_to_all(values, axis, 0, 0, tiled=True)  30.5 us
    all_gather x1, blocking collectives, on_device(): normed_all = lax.all_gather(normed, 'seq', axis=0, tiled=True)  30.2 us
    all_to_all x2, blocking collectives, exchange(): return lax.all_to_all(values, axis, 0, 0, tiled=True)  29.8 us
    all_gather x1, blocking collectives, on_device(): qkv_rows = lax.all_gather(qkv_cols, 'seq', axis=1, tiled=True)  28.8 us
    psum x1, blocking collectives, on_device(): square_sum = lax.psum(jnp.sum(x_home * x_home, axis=-1), 'mp')  27.4 us
    all_to_all x1, waiting for transfers between devices, on_device(): lax.all_to_all(jnp.stack([mine_x for _ in range(lax.axis_size('mp'))], 0)...  10.2 us
  transfers between devices with their start and end apart: 6, of which 6 were waited for; matrix products, arithmetic and copies ran while one was open for 5% of the time, Pallas kernels for 0%

profile of v1, /device:TPU:1, one launch (start us, length us, event | category | flops | bytes accessed | tf_op | source)
XLA Modules:
  0.0 329.5 jit_solution(2485919629909847429)
XLA Ops:
  0.0 0.7 compare_and_fusion.1
  0.7 0.7 subtract_clamp_fusion
  2.2 2.2 copy.149
  4.4 3.2 gather_fusion
  7.6 1.0 select_select_fusion
  8.7 10.4 %all-to-all-start = ((bf16[32,32,96]{2,1,0:T(8,128)(2,1)}), bf16[32,32,96]{2,1,0:T(8,128)(2,1)S(1)}, u32[]{:S(2)}, u32[]{:S(2)}) async-start(bf16[32,32,96]{2,1,0:T(8,128)(2,1)} %select_select_fusion), calls=%async_computation | async-start | bytes 524288 | tf_op jit(solution)/shard_map/all_to_all | solution.py:21
  19.0 0.5 iota_compare_fusion.2
  19.6 0.5 compare_and_fusion.2
  20.1 0.6 subtract_compare_fusion
  20.7 0.6 fusion.76
  22.9 1.3 broadcast_select_fusion.2
  24.2 3.9 %all-to-all-done = bf16[32,32,96]{2,1,0:T(8,128)(2,1)S(1)} async-done(((bf16[32,32,96]{2,1,0:T(8,128)(2,1)}), bf16[32,32,96]{2,1,0:T(8,128)(2,1)S(1)}, u32[]{:S(2)}, u32[]{:S(2)}) %all-to-all-start) | async-done | bytes 196640 | tf_op jit(solution)/shard_map/all_to_all | solution.py:21
  28.3 27.4 %psum.7 = f32[32]{0:T(128)S(1)} all-reduce(f32[32]{0:T(128)S(1)} %multiply_reduce_fusion.2), channel_id=1, replica_groups=mesh['seq'=32,'mp'=16] {'mp'}, use_global_device_ids=true, to_apply=%region_2.3 | all-reduce | flops 32 | bytes 256 | tf_op jit(solution)/shard_map/psum | solution.py:54
  55.7 30.2 %all_gather.9 = bf16[1024,96]{1,0:T(8,128)(2,1)S(1)} all-gather(bf16[32,96]{1,0:T(8,128)(2,1)S(1)} %multiply_convert_fusion), channel_id=1, replica_groups=mesh['seq'=32,'mp'=16] {'seq'}, dimensions={0}, use_global_device_ids=true | all-gather | bytes 202752 | tf_op jit(solution)/shard_map/all_gather | solution.py:56
  86.5 1.0 reshape.314
  87.5 6.4 %all-to-all-start.1 = ((f32[16,1,4096]{2,1,0:T(1,128)}), f32[16,1,4096]{2,1,0:T(1,128)S(1)}, u32[]{:S(2)}, u32[]{:S(2)}) async-start(f32[16,1,4096]{2,1,0:T(1,128)} %reshape.314), calls=%async_computation.1 | async-start | bytes 524288 | tf_op jit(solution)/shard_map/all_to_all | solution.py:21
  94.2 0.6 pad_clamp_fusion
  94.9 13.2 %all-to-all-done.1 = f32[16,1,4096]{2,1,0:T(1,128)S(1)} async-done(((f32[16,1,4096]{2,1,0:T(1,128)}), f32[16,1,4096]{2,1,0:T(1,128)S(1)}, u32[]{:S(2)}, u32[]{:S(2)}) %all-to-all-start.1) | async-done | bytes 262176 | tf_op jit(solution)/shard_map/all_to_all | solution.py:21
  108.1 0.6 broadcast.248
  108.7 1.2 reduce.3
  110.2 28.8 %all_gather.10 = bf16[64,2048]{0,1:T(8,128)(2,1)S(1)} all-gather(bf16[64,64]{0,1:T(8,128)(2,1)S(1)} %bitcast_reduce_fusion), channel_id=1, replica_groups=mesh['seq'=32,'mp'=16] {'seq'}, dimensions={1}, use_global_device_ids=true | all-gather | bytes 270336 | tf_op jit(solution)/shard_map/all_gather | solution.py:61
  139.1 0.6 fusion.74
  140.0 0.6 reshape.246
  140.8 0.8 fusion.77
  141.9 0.5 fusion.34
  142.4 0.4 convolution_bitcast_fusion.1
  143.4 0.6 gather_fusion.1
  144.0 0.6 gather_fusion.2
  144.6 0.4 reshape_reshape.3
  145.1 1.0 copy.166
  146.0 1.0 copy.163
  147.0 1.6 pad_maximum_fusion
  148.6 1.8 copy.167
  150.5 1.3 reshape.316
  151.8 4.3 %all-to-all-start.2 = ((f32[32,1,3328]{2,1,0:T(1,128)}), f32[32,1,3328]{2,1,0:T(1,128)S(1)}, u32[]{:S(2)}, u32[]{:S(2)}) async-start(f32[32,1,3328]{2,1,0:T(1,128)} %reshape.316), calls=%async_computation.2 | async-start | bytes 851968 | tf_op jit(solution)/shard_map/all_to_all | solution.py:21
  156.1 1.3 fusion.78
  158.6 0.7 gather_fusion.4
  159.3 0.7 gather_fusion.3
  160.7 5.9 %all-to-all-done.2 = f32[32,1,3328]{2,1,0:T(1,128)S(1)} async-done(((f32[32,1,3328]{2,1,0:T(1,128)}), f32[32,1,3328]{2,1,0:T(1,128)S(1)}, u32[]{:S(2)}, u32[]{:S(2)}) %all-to-all-start.2) | async-done | bytes 426016 | tf_op jit(solution)/shard_map/all_to_all | solution.py:21
  166.6 1.6 reduce.4
  169.4 0.8 reshape.318
  170.2 5.8 %all-to-all-start.3 = ((bf16[16,2,1536]{2,1,0:T(2,128)(2,1)}), bf16[16,2,1536]{2,1,0:T(2,128)(2,1)S(1)}, u32[]{:S(2)}, u32[]{:S(2)}) async-start(bf16[16,2,1536]{2,1,0:T(2,128)(2,1)} %reshape.318), calls=%async_computation.3 | async-start | bytes 196608 | tf_op jit(solution)/shard_map/all_to_all | solution.py:140
  176.0 0.8 fusion.1
  176.8 0.5 copy.192
  177.6 0.6 copy.194
  178.1 10.2 %all-to-all-done.3 = bf16[16,2,1536]{2,1,0:T(2,128)(2,1)S(1)} async-done(((bf16[16,2,1536]{2,1,0:T(2,128)(2,1)}), bf16[16,2,1536]{2,1,0:T(2,128)(2,1)S(1)}, u32[]{:S(2)}, u32[]{:S(2)}) %all-to-all-start.3) | async-done | bytes 98336 | tf_op jit(solution)/shard_map/all_to_all | solution.py:140
  188.7 1.0 fusion.63
  189.7 5.4 %all-to-all-start.4 = ((f32[32,32,96]{2,1,0:T(8,128)}), f32[32,32,96]{2,1,0:T(8,128)S(1)}, u32[]{:S(2)}, u32[]{:S(2)}) async-start(f32[32,32,96]{2,1,0:T(8,128)} %fusion.63), calls=%async_computation.4 | async-start | bytes 1048576 | tf_op jit(solution)/shard_map/all_to_all | solution.py:21
  195.1 0.9 fusion
  196.0 0.9 copy-done.4
  197.1 9.6 %all-to-all-done.4 = f32[32,32,96]{2,1,0:T(8,128)S(1)} async-done(((f32[32,32,96]{2,1,0:T(8,128)}), f32[32,32,96]{2,1,0:T(8,128)S(1)}, u32[]{:S(2)}, u32[]{:S(2)}) %all-to-all-start.4) | async-done | bytes 393248 | tf_op jit(solution)/shard_map/all_to_all | solution.py:21
  207.0 10.8 %all_to_all.40 = bf16[32,8,96]{2,1,0:T(8,128)(2,1)S(1)} all-to-all(bf16[32,8,96]{2,1,0:T(8,128)(2,1)S(1)} %copy.196), channel_id=1, replica_groups=mesh['seq'=32,'mp'=16] {'seq'}, dimensions={0} | all-to-all | bytes 98304 | tf_op jit(solution)/shard_map/all_to_all | solution.py:21
  217.8 0.8 copy.197
  218.6 46.6 %all_gather.11 = bf16[32,8,1536]{0,1,2:T(8,128)(2,1)S(1)} all-gather(bf16[32,8,96]{0,1,2:T(8,128)(2,1)} %copy.197), channel_id=1, replica_groups=mesh['seq'=32,'mp'=16] {'mp'}, dimensions={2}, use_global_device_ids=true | all-gather | bytes 835584 | tf_op jit(solution)/shard_map/all_gather | solution.py:165
  265.2 3.6 %copy.198 = bf16[32,8,1536]{2,1,0:T(8,128)(2,1)} copy(bf16[32,8,1536]{0,1,2:T(8,128)(2,1)S(1)} %all_gather.11) | data formatting | bytes 1572864 | tf_op jit(solution)/shard_map/all_gather | solution.py:165
  268.9 1.4 fusion.5
  270.5 1.6 fusion.24
  272.5 1.2 copy.203
  273.6 4.1 %all-to-all-start.6 = ((bf16[16,256,96]{1,2,0:T(8,128)(2,1)}), bf16[16,256,96]{1,2,0:T(8,128)(2,1)S(1)}, u32[]{:S(2)}, u32[]{:S(2)}) async-start(bf16[16,256,96]{1,2,0:T(8,128)(2,1)} %bitcast.39), calls=%async_computation.6 | async-start | bytes 1572864 | tf_op jit(solution)/shard_map/all_to_all | solution.py:21
  277.8 1.0 multiply_reduce_fusion
  279.0 0.4 multiply_reduce_fusion.1
  279.7 29.7 %all-to-all-done.6 = bf16[16,256,96]{1,2,0:T(8,128)(2,1)S(1)} async-done(((bf16[16,256,96]{1,2,0:T(8,128)(2,1)}), bf16[16,256,96]{1,2,0:T(8,128)(2,1)S(1)}, u32[]{:S(2)}, u32[]{:S(2)}) %all-to-all-start.6) | async-done | bytes 786464 | tf_op jit(solution)/shard_map/all_to_all | solution.py:21
  309.7 19.0 %all_to_all.41 = bf16[32,8,96]{2,1,0:T(8,128)(2,1)S(1)} all-to-all(bf16[32,8,96]{2,1,0:T(8,128)(2,1)S(1)} %fusion.46), channel_id=1, replica_groups=mesh['seq'=32,'mp'=16] {'seq'}, dimensions={0} | all-to-all | bytes 98304 | tf_op jit(solution)/shard_map/all_to_all | solution.py:21
  328.7 0.8 fusion.13
  (143 shorter events, 10.2 us)
Async XLA Ops:
  0.0 270.5 %copy-start = (bf16[1,2,48,1536]{3,2,1,0:T(8,128)(2,1)S(1)}, bf16[1,2,48,1536]{3,2,1,0:T(8,128)(2,1)}, u32[]{:S(2)}) copy-start(bf16[1,2,48,1536]{3,2,1,0:T(8,128)(2,1)} %param.32) | copy-start | bytes 884740
  4.4 16.3 %copy-start.18 = (s32[2]{0:T(128)S(1)}, s32[2]{0:T(128)}, u32[]{:S(2)}) copy-start(s32[2]{0:T(128)} %param.28) | copy-start | bytes 28
  4.4 17.0 %copy-start.10 = (bf16[2,2,64,256]{3,2,1,0:T(8,128)(2,1)S(1)}, bf16[2,2,64,256]{3,2,1,0:T(8,128)(2,1)}, u32[]{:S(2)}) copy-start(bf16[2,2,64,256]{3,2,1,0:T(8,128)(2,1)} %param.25) | copy-start | bytes 393220
  4.4 17.1 %copy-start.12 = (s32[256,4,4]{0,2,1:T(4,128)S(1)}, s32[256,4,4]{0,2,1:T(4,128)}, u32[]{:S(2)}) copy-start(s32[256,4,4]{0,2,1:T(4,128)} %param.34) | copy-start | bytes 49156
  7.6 14.4 %copy-start.5 = (bf16[2,16,64,256]{3,2,1,0:T(8,128)(2,1)S(1)}, bf16[2,16,64,256]{3,2,1,0:T(8,128)(2,1)}, u32[]{:S(2)}) copy-start(bf16[2,16,64,256]{3,2,1,0:T(8,128)(2,1)} %param.26) | copy-start | bytes 3145732
  8.7 19.4 %all-to-all-start = ((bf16[32,32,96]{2,1,0:T(8,128)(2,1)}), bf16[32,32,96]{2,1,0:T(8,128)(2,1)S(1)}, u32[]{:S(2)}, u32[]{:S(2)}) async-start(bf16[32,32,96]{2,1,0:T(8,128)(2,1)} %select_select_fusion), calls=%async_computation | async-start | bytes 524288 | tf_op jit(solution)/shard_map/all_to_all | solution.py:21
  22.2 0.7 copy-start.21
  22.2 33.4 %copy-start.19 = (f32[96]{0:T(128)S(1)}, f32[96]{0:T(128)}, u32[]{:S(2)}) copy-start(f32[96]{0:T(128)} %param.22) | copy-start | bytes 1156
  22.4 63.6 %copy-start.13 = (bf16[96,64]{0,1:T(8,128)(2,1)S(1)}, bf16[96,64]{0,1:T(8,128)(2,1)}, u32[]{:S(2)}) copy-start(bf16[96,64]{0,1:T(8,128)(2,1)} %param.23) | copy-start | bytes 36868
  86.2 7.8 %copy-start.22 = (s32[16]{0:T(128)S(1)}, s32[16]{0:T(128)}, u32[]{:S(2)}) copy-start(s32[16]{0:T(128)} %param.29) | copy-start | bytes 196
  86.2 8.6 %copy-start.20 = (s32[64]{0:T(128)S(1)}, s32[64]{0:T(128)}, u32[]{:S(2)}) copy-start(s32[64]{0:T(128)} %constant.117) | copy-start | bytes 772
  87.5 20.6 %all-to-all-start.1 = ((f32[16,1,4096]{2,1,0:T(1,128)}), f32[16,1,4096]{2,1,0:T(1,128)S(1)}, u32[]{:S(2)}, u32[]{:S(2)}) async-start(f32[16,1,4096]{2,1,0:T(1,128)} %reshape.314), calls=%async_computation.1 | async-start | bytes 524288 | tf_op jit(solution)/shard_map/all_to_all | solution.py:21
  140.8 1.6 copy-start.6
  150.5 5.6 %copy-start.7 = (bf16[16,4,2,6,128]{4,3,2,1,0:T(8,128)(2,1)S(1)}, bf16[16,4,2,6,128]{4,3,2,1,0:T(8,128)(2,1)}, u32[]{:S(2)}) copy-start(bf16[16,4,2,6,128]{4,3,2,1,0:T(8,128)(2,1)} %copy-done.6) | copy-start | bytes 589828
  150.5 5.6 %copy-start.11 = (bf16[16,4,2,128]{3,2,1,0:T(2,128)(2,1)S(1)}, bf16[16,4,2,128]{3,2,1,0:T(2,128)(2,1)}, u32[]{:S(2)}) copy-start(bf16[16,4,2,128]{3,2,1,0:T(2,128)(2,1)} %reshape.246) | copy-start | bytes 98308
  150.5 5.6 %copy-start.16 = (pred[4,4]{1,0:T(4,128)(4,1)S(1)}, pred[4,4]{1,0:T(4,128)(4,1)}, u32[]{:S(2)}) copy-start(pred[4,4]{1,0:T(4,128)(4,1)} %iota_compare_fusion.2) | copy-start | bytes 52
  150.5 7.5 %copy-start.8 = (bf16[64,256]{0,1:T(8,128)(2,1)S(1)}, bf16[64,256]{0,1:T(8,128)(2,1)}, u32[]{:S(2)}) copy-start(bf16[64,256]{0,1:T(8,128)(2,1)} %get-tuple-element.16) | copy-start | bytes 98308
  151.8 14.9 %all-to-all-start.2 = ((f32[32,1,3328]{2,1,0:T(1,128)}), f32[32,1,3328]{2,1,0:T(1,128)S(1)}, u32[]{:S(2)}, u32[]{:S(2)}) async-start(f32[32,1,3328]{2,1,0:T(1,128)} %reshape.316), calls=%async_computation.2 | async-start | bytes 851968 | tf_op jit(solution)/shard_map/all_to_all | solution.py:21
  160.4 8.2 %copy-start.17 = (pred[48]{0:T(512)(128)(4,1)S(1)}, pred[48]{0:T(512)(128)(4,1)}, u32[]{:S(2)}) copy-start(pred[48]{0:T(512)(128)(4,1)} %subtract_compare_fusion) | copy-start | bytes 148
  160.4 8.3 %copy-start.15 = (pred[48]{0:T(512)(128)(4,1)S(1)}, pred[48]{0:T(512)(128)(4,1)}, u32[]{:S(2)}) copy-start(pred[48]{0:T(512)(128)(4,1)} %compare_and_fusion.2) | copy-start | bytes 148
  170.2 18.5 %copy-start.14 = (bf16[48,96]{1,0:T(8,128)(2,1)S(1)}, bf16[48,96]{1,0:T(8,128)(2,1)}, u32[]{:S(2)}) copy-start(bf16[48,96]{1,0:T(8,128)(2,1)} %param.24) | copy-start | bytes 27652
  170.2 18.1 %all-to-all-start.3 = ((bf16[16,2,1536]{2,1,0:T(2,128)(2,1)}), bf16[16,2,1536]{2,1,0:T(2,128)(2,1)S(1)}, u32[]{:S(2)}, u32[]{:S(2)}) async-start(bf16[16,2,1536]{2,1,0:T(2,128)(2,1)} %reshape.318), calls=%async_computation.3 | async-start | bytes 196608 | tf_op jit(solution)/shard_map/all_to_all | solution.py:140
  176.8 0.6 copy-start.2
  189.7 17.0 %all-to-all-start.4 = ((f32[32,32,96]{2,1,0:T(8,128)}), f32[32,32,96]{2,1,0:T(8,128)S(1)}, u32[]{:S(2)}, u32[]{:S(2)}) async-start(f32[32,32,96]{2,1,0:T(8,128)} %fusion.63), calls=%async_computation.4 | async-start | bytes 1048576 | tf_op jit(solution)/shard_map/all_to_all | solution.py:21
  196.0 1.0 copy-start.4
  265.2 5.2 %copy-start.24 = (f32[1536]{0:T(1024)S(1)}, f32[1536]{0:T(1024)}, u32[]{:S(2)}) copy-start(f32[1536]{0:T(1024)} %param.30) | copy-start | bytes 18436
  268.9 3.2 copy-start.9
  272.4 5.3 %copy-start.3 = (pred[32,32,32]{2,1,0:T(8,128)(4,1)S(1)}, pred[32,32,32]{2,1,0:T(8,128)(4,1)}, u32[]{:S(2)}) copy-start(pred[32,32,32]{2,1,0:T(8,128)(4,1)} %copy-done.2) | copy-start | bytes 98308
  272.5 6.5 %copy-start.1 = (bf16[32,8,1536]{2,1,0:T(8,128)(2,1)S(1)}, bf16[32,8,1536]{2,1,0:T(8,128)(2,1)}, u32[]{:S(2)}) copy-start(bf16[32,8,1536]{2,1,0:T(8,128)(2,1)} %copy.198) | copy-start | bytes 2359300
  272.5 6.5 %copy-start.23 = (bf16[1536,32]{0,1:T(8,128)(2,1)S(1)}, bf16[1536,32]{0,1:T(8,128)(2,1)}, u32[]{:S(2)}) copy-start(bf16[1536,32]{0,1:T(8,128)(2,1)} %param.31) | copy-start | bytes 294916
  273.6 35.7 %all-to-all-start.6 = ((bf16[16,256,96]{1,2,0:T(8,128)(2,1)}), bf16[16,256,96]{1,2,0:T(8,128)(2,1)S(1)}, u32[]{:S(2)}, u32[]{:S(2)}) async-start(bf16[16,256,96]{1,2,0:T(8,128)(2,1)} %bitcast.39), calls=%async_computation.6 | async-start | bytes 1572864 | tf_op jit(solution)/shard_map/all_to_all | solution.py:21
